TPU v7x, 256 devices: a whole 4x4x8 slice. The times are simulated.
256 devices in a mesh: dp: 64 (over z, x, core), mp: 4 (over y).
Axes of the slice: x: 4, y: 4, z: 8, core: 2. Of those that a mesh axis runs over, the one named last changes fastest.
Arguments:
- embed_table: float32 [16, 32768, 256], P('mp', 'dp'), may hold values from -5 to 5
- accum: float32 [16, 32768], P('mp', 'dp'), may hold values from 0.1 to 3
- stale_grad: bfloat16 [16, 32768, 256], P('mp', 'dp'), may hold values from -6 to 6
- grad_owner: int32 [16, 32768, 1], P('mp', 'dp'), may hold values from 0 to 63; in each aligned block of 512 rows (0 to 511, 512 to 1023, ..., all dimensions but the last counted through in order) at most 16 rows name the same one
- grad_row: int32 [16, 32768], P('mp', 'dp'), may hold values from 0 to 511
- lookup_owner: int32 [16, 32768, 1], P('mp', 'dp'), may hold values from 0 to 63; in each aligned block of 512 rows (0 to 511, 512 to 1023, ..., all dimensions but the last counted through in order) at most 16 rows name the same one
- lookup_row: int32 [16, 32768], P('mp', 'dp'), may hold values from 0 to 511
- bag_len: int32 [16, 16384], P('mp', 'dp'), may hold values from 1 to 2
- label: int32 [16384], P('dp'), may hold values 0 or 1
- up_factor_weight: bfloat16 [2, 512, 4096], P(None, None, 'mp'), may hold values from -0.25 to 0.25
- v_weight: bfloat16 [2, 512, 4096], P(None, None, 'mp'), may hold values from -0.09375 to 0.09375
- cross_bias: float32 [2, 4096], P(None, 'mp'), may hold values from -3 to 3
- head_weight: float32 [4096], P('mp'), may hold values from -0.09375 to 0.09375
Outputs:
- new_table: float32 [16, 32768, 256], P('mp', 'dp')
- new_accum: float32 [16, 32768], P('mp', 'dp')
- grad_u: float32 [2, 512, 4096], P(None, 'dp', 'mp')
- grad_v: float32 [2, 512, 4096], P(None, 'dp', 'mp')
- grad_small: float32 [3, 4096], P(None, 'mp')
- grad_pooled: bfloat16 [16384, 4096], P('dp', 'mp')
Inputs may be any that keep to these rules, and one draw needn't show every extreme that they name: `grad_owner`: among the 512 blocks of one feature held by one index of dp, at most 16 name the same owner, and in some such group exactly 16 do. `lookup_owner`: among the 512 id slots of one feature belonging to one index of dp, at most 16 name the same owner, and in some such group exactly 16 do; slots k >= bag_len are unused.
All inputs are finite; a program needn't handle non-finite values. No bound on the sum of `label` on one device may be relied on, other than what follows from the above.
Results may differ from a plain program's by a relative error of at most 0.009.
Values may be sent and summed in bfloat16 or wider, within the bound.
No kernel may reach another device: no remote copies, remote signals or barrier semaphores. Data moves between devices by JAX's collectives and lax.ppermute only.
A program may use at most 128 MiB of HBM per device.

v0:
```python
import jax
import jax.numpy as jnp
from jax import lax
from jax.sharding import PartitionSpec as P

learn_rate = 0.5


def in_blocks(array, dim, devices):
    shape = array.shape
    parts = array.reshape(*shape[:dim], devices, shape[dim] // devices, *shape[dim + 1 :])
    return jnp.moveaxis(parts, dim, 0)


def sum_at_owner(array, axis, dim):
    parts = in_blocks(array, dim, lax.axis_size(axis))
    arrived = lax.all_to_all(parts, axis, split_axis=0, concat_axis=0, tiled=True)
    return arrived.sum(axis=0)


def copy_for_each(array, axis):
    copies = jnp.broadcast_to(array, (lax.axis_size(axis), *array.shape))
    return lax.all_to_all(copies, axis, split_axis=0, concat_axis=0, tiled=True)


def over_copies(array, axis):
    return copy_for_each(array, axis).sum(axis=0)


def side_by_side(arrays, axis, dim, along):
    widths = [a.shape[along] for a in arrays]
    both = jnp.concatenate(arrays, axis=along)
    filled = lax.psum_scatter(both, axis, scatter_dimension=dim, tiled=True)
    return tuple(jnp.split(filled, [sum(widths[:k]) for k in range(1, len(widths))], axis=along))


def bucket_slots(owners, capacity, peers):
    count = owners.shape[1]
    onehot = (owners[:, None, :] == jnp.arange(peers)[None, :, None]).astype(jnp.bfloat16)
    earlier = (jnp.arange(count)[:, None] < jnp.arange(count)[None, :]).astype(jnp.bfloat16)
    before = jnp.einsum("fpi,ij->fpj", onehot, earlier, preferred_element_type=jnp.float32)
    order_in = jnp.sum(before * onehot.astype(jnp.float32), axis=1)
    return owners * capacity + order_in.astype(jnp.int32)


def selection_matrix(indices, length):
    return (indices[:, :, None] == jnp.arange(length)[None, None, :]).astype(jnp.bfloat16)


def contract_last(left, right):
    return lax.dot_general(
        left, right, (((1,), (1,)), ((), ())), preferred_element_type=jnp.float32
    )


def contract_first(left, right):
    return lax.dot_general(
        left, right, (((0,), (0,)), ((), ())), preferred_element_type=jnp.float32
    )


def summed_rounded(partial, axis):
    share = lax.psum_scatter(partial, axis, scatter_dimension=0, tiled=True)
    return lax.all_gather(share.astype(jnp.bfloat16), axis, axis=0, tiled=True)


def cross_down(state, v_layer):
    return summed_rounded(contract_last(state, v_layer), "mp")


def local(
    embed_table,
    accum,
    stale_grad,
    grad_owner,
    grad_row,
    lookup_owner,
    lookup_row,
    bag_len,
    label,
    up_factor_weight,
    v_weight,
    cross_bias,
    head_weight,
):
    peers = lax.axis_size("dp")
    local_feats, grad_dev, width = stale_grad.shape
    rows_per_shard = embed_table.shape[1]
    which_feature = jnp.arange(local_feats)[:, None]
    grad_cap = max(2, 2 * grad_dev // peers)
    grad_total = peers * grad_cap
    grad_slot = bucket_slots(grad_owner[:, :, 0], grad_cap, peers)
    place = selection_matrix(grad_slot, grad_total)
    send_grads = jnp.einsum(
        "fns,fne->fse", place, stale_grad, preferred_element_type=jnp.float32
    ).astype(jnp.bfloat16)
    send_rows = (
        jnp.full((local_feats, grad_total), rows_per_shard, jnp.int32)
        .at[which_feature, grad_slot]
        .set(grad_row)
    )
    recv_grads = lax.all_to_all(
        send_grads.reshape(local_feats, peers, grad_cap, width),
        "dp",
        split_axis=1,
        concat_axis=1,
        tiled=True,
    )
    recv_rows = lax.all_to_all(
        send_rows.reshape(local_feats, peers, grad_cap),
        "dp",
        split_axis=1,
        concat_axis=1,
        tiled=True,
    )
    landing = selection_matrix(recv_rows.reshape(local_feats, grad_total), rows_per_shard)
    summed = jnp.einsum(
        "wjc,wjl->wcl",
        landing,
        recv_grads.reshape(local_feats, grad_total, width),
        preferred_element_type=jnp.float32,
    )
    new_accum = accum + jnp.mean(summed * summed, axis=2)
    new_table = embed_table - learn_rate * summed / jnp.sqrt(new_accum)[:, :, None]
    batch_dev = bag_len.shape[1]
    look_dev = lookup_row.shape[1]
    bag_size = look_dev // batch_dev
    look_cap = max(2, 2 * look_dev // peers)
    look_total = peers * look_cap
    look_slot = bucket_slots(lookup_owner[:, :, 0], look_cap, peers)
    wanted = (
        jnp.zeros((local_feats, look_total), jnp.int32).at[which_feature, look_slot].set(lookup_row)
    )
    requested_ids = lax.all_to_all(
        wanted.reshape(local_feats, peers, look_cap), "dp", split_axis=1, concat_axis=1, tiled=True
    ).reshape(local_feats, look_total)
    second_table = embed_table.astype(jnp.bfloat16)
    served = jnp.einsum(
        "adv,avm->adm",
        selection_matrix(requested_ids, rows_per_shard),
        second_table,
        preferred_element_type=jnp.float32,
    ).astype(jnp.bfloat16)
    returned = lax.all_to_all(
        served.reshape(local_feats, peers, look_cap, width),
        "dp",
        split_axis=1,
        concat_axis=1,
        tiled=True,
    ).reshape(local_feats, look_total, width)
    slots = look_slot.reshape(local_feats, batch_dev, bag_size)
    mixing = jnp.zeros((local_feats, batch_dev, look_total), jnp.bfloat16)
    for member in range(bag_size):
        used = (bag_len > member).astype(jnp.bfloat16)
        mixing = mixing + selection_matrix(slots[:, :, member], look_total) * used[:, :, None]
    pooled = jnp.einsum(
        "fbs,fse->fbe", mixing, returned, preferred_element_type=jnp.float32
    ).astype(jnp.bfloat16)
    start = jnp.transpose(pooled, (1, 0, 2)).reshape(batch_dev, local_feats * width)
    start_f = start.astype(jnp.float32)
    n_layers = up_factor_weight.shape[0]
    state = start
    states = []
    downs = []
    crosses = []
    for layer in range(n_layers):
        down_sum = cross_down(state, v_weight[layer])
        cross_out = (
            jnp.dot(down_sum, up_factor_weight[layer], preferred_element_type=jnp.float32)
            + cross_bias[layer]
        )
        states.append(state)
        downs.append(down_sum)
        crosses.append(cross_out)
        state = (start_f * cross_out + state.astype(jnp.float32)).astype(jnp.bfloat16)
    logit = lax.psum(jnp.sum(state.astype(jnp.float32) * head_weight[None, :], axis=1), "mp")
    slope = (jax.nn.sigmoid(logit) - label.astype(jnp.float32)) / jnp.sqrt(
        jnp.float32(batch_dev * peers)
    )
    upstream = slope[:, None] * head_weight[None, :]
    head_grad = jnp.sum(slope[:, None] * state.astype(jnp.float32), axis=0)
    to_start = jnp.zeros(start_f.shape, jnp.float32)
    grads_u = [None] * n_layers
    grads_v = [None] * n_layers
    bias_grads = [None] * n_layers
    for layer in reversed(range(n_layers)):
        direct = upstream * start_f
        bias_grads[layer] = jnp.sum(direct, axis=0)
        direct_bias_term = direct.astype(jnp.bfloat16)
        grad_u_layer = contract_first(downs[layer], direct_bias_term)
        back_sum = summed_rounded(contract_last(direct_bias_term, up_factor_weight[layer]), "mp")
        down_factor_gradient = contract_first(back_sum, states[layer])
        to_start = to_start + upstream * crosses[layer]
        upstream = upstream + jnp.dot(back_sum, v_weight[layer], preferred_element_type=jnp.float32)
        grads_u[layer] = grad_u_layer
        grads_v[layer] = down_factor_gradient
    grad_u = jnp.stack(grads_u)
    grad_v = jnp.stack(grads_v)
    grad_u, grad_v = side_by_side((grad_u, grad_v), "dp", 1, 0)
    grad_small = lax.psum(jnp.stack(bias_grads + [head_grad]), "dp")
    grad_pooled = (upstream + to_start).astype(jnp.bfloat16)
    return (new_table, new_accum, grad_u, grad_v, grad_small, grad_pooled)


def solution(mesh):
    return jax.shard_map(
        local,
        mesh=mesh,
        in_specs=(
            P("mp", "dp", None),
            P("mp", "dp"),
            P("mp", "dp", None),
            P("mp", "dp", None),
            P("mp", "dp"),
            P("mp", "dp", None),
            P("mp", "dp"),
            P("mp", "dp"),
            P("dp"),
            P(None, None, "mp"),
            P(None, None, "mp"),
            P(None, "mp"),
            P("mp"),
        ),
        out_specs=(
            P("mp", "dp", None),
            P("mp", "dp"),
            P(None, "dp", "mp"),
            P(None, "dp", "mp"),
            P(None, "mp"),
            P("dp", "mp"),
        ),
        check_vma=False,
    )
```

profile of v0, /device:TPU:0, one launch (start us, length us, event | category | flops | bytes accessed | tf_op | source)
XLA Modules:
  0.0 633.7 jit_solution(6955148603846393421)
XLA Ops:
  10.6 8.1 %scatter_custom_fusion.1 = s32[4096]{0:T(1024)S(1)} fusion(s32[2048]{0:T(1024)S(1)} %bitcast.111, s32[2048]{0:T(1024)S(1)} %bitcast.113, s32[]{:T(128)} %constant.5.clone.1), kind=kCustom, calls=%fused_computation.105 | custom fusion | bytes 16388
  18.9 21.1 %all_to_all.20 = s32[4,64,16]{2,0,1:T(4,128)S(1)} all-to-all(s32[4,64,16]{2,0,1:T(4,128)S(1)} %copy.43), channel_id=1, replica_groups=mesh['dp'=64,'mp'=4] {'dp'}, dimensions={1} | all-to-all | bytes 32768 | tf_op jit(solution)/shard_map/all_to_all | solution.py:134
  43.8 4.7 all-to-all-start.3
  51.0 48.8 %all-to-all-done.3 = bf16[4,64,16,256]{3,2,0,1:T(8,128)(2,1)S(1)} async-done(((bf16[4,64,16,256]{3,2,0,1:T(8,128)(2,1)}), bf16[4,64,16,256]{3,2,0,1:T(8,128)(2,1)S(1)}, u32[]{:S(2)}, u32[]{:S(2)}) %all-to-all-start.3) | async-done | bytes 2097184 | tf_op jit(solution)/shard_map/all_to_all | solution.py:144
  103.7 20.2 %reduce-scatter.6.cloned.1.call-done = f32[64,512]{1,0:T(8,128)} async-done(((f32[256,512]{1,0:T(8,128)}), f32[64,512]{1,0:T(8,128)}) %reduce-scatter.6.cloned.1.call-update) | async-done | bytes 131088 | tf_op jit(solution)/shard_map/reduce_scatter | solution.py:63
  125.0 12.3 %all_gather.12 = bf16[256,512]{1,0:T(8,128)(2,1)S(1)} all-gather(bf16[64,512]{1,0:T(8,128)(2,1)S(1)} %convert_element_type.138), channel_id=1, replica_groups=mesh['dp'=64,'mp'=4] {'mp'}, dimensions={0}, use_global_device_ids=true | all-gather | bytes 327680 | tf_op jit(solution)/shard_map/all_gather | solution.py:64
  141.5 23.9 %reduce-scatter.8.cloned.1.call-done = f32[64,512]{1,0:T(8,128)} async-done(((f32[256,512]{1,0:T(8,128)}), f32[64,512]{1,0:T(8,128)}) %reduce-scatter.8.cloned.1.call-update) | async-done | bytes 131088 | tf_op jit(solution)/shard_map/reduce_scatter | solution.py:63
  166.3 12.3 %all_gather.13 = bf16[256,512]{1,0:T(8,128)(2,1)S(1)} all-gather(bf16[64,512]{1,0:T(8,128)(2,1)S(1)} %convert_element_type.141), channel_id=1, replica_groups=mesh['dp'=64,'mp'=4] {'mp'}, dimensions={0}, use_global_device_ids=true | all-gather | bytes 327680 | tf_op jit(solution)/shard_map/all_gather | solution.py:64
  178.5 2.9 fusion.23
  181.4 8.4 %psum.14 = f32[256]{0:T(256)S(1)} all-reduce(f32[256]{0:T(256)S(1)} %get-tuple-element.28), channel_id=1, replica_groups=mesh['dp'=64,'mp'=4] {'mp'}, use_global_device_ids=true, to_apply=%region_8.0 | all-reduce | flops 256 | bytes 2048 | tf_op jit(solution)/shard_map/psum | solution.py:176
  192.8 23.7 %reduce-scatter.10.cloned.1.call-done = f32[64,512]{1,0:T(8,128)} async-done(((f32[256,512]{1,0:T(8,128)}), f32[64,512]{1,0:T(8,128)}) %reduce-scatter.10.cloned.1.call-update) | async-done | bytes 131088 | tf_op jit(solution)/shard_map/reduce_scatter | solution.py:63
  217.5 12.3 %all_gather.14 = bf16[256,512]{1,0:T(8,128)(2,1)S(1)} all-gather(bf16[64,512]{1,0:T(8,128)(2,1)S(1)} %convert_element_type.149), channel_id=1, replica_groups=mesh['dp'=64,'mp'=4] {'mp'}, dimensions={0}, use_global_device_ids=true | all-gather | bytes 327680 | tf_op jit(solution)/shard_map/all_gather | solution.py:64
  239.3 18.1 %reduce-scatter.12.cloned.1.call-done = f32[64,512]{1,0:T(8,128)} async-done(((f32[256,512]{1,0:T(8,128)}), f32[64,512]{1,0:T(8,128)}) %reduce-scatter.12.cloned.1.call-update) | async-done | bytes 131088 | tf_op jit(solution)/shard_map/reduce_scatter | solution.py:63
  258.5 12.3 %all_gather.15 = bf16[256,512]{1,0:T(8,128)(2,1)S(1)} all-gather(bf16[64,512]{1,0:T(8,128)(2,1)S(1)} %convert_element_type.152), channel_id=1, replica_groups=mesh['dp'=64,'mp'=4] {'mp'}, dimensions={0}, use_global_device_ids=true | all-gather | bytes 327680 | tf_op jit(solution)/shard_map/all_gather | solution.py:64
  271.2 5.2 pad_maximum_fusion
  277.1 8.1 %scatter_custom_fusion = s32[4096]{0:T(1024)S(1)} fusion(s32[2048]{0:T(1024)S(1)} %bitcast.112, s32[2048]{0:T(1024)S(1)} %bitcast.114, s32[]{:T(128)} %constant.11.clone.1), kind=kCustom, calls=%fused_computation.107 | custom fusion | bytes 16388
  286.0 10.4 %all-to-all-start = ((s32[4,64,16]{2,0,1:T(4,128)}), s32[4,64,16]{2,0,1:T(4,128)S(1)}, u32[]{:S(2)}, u32[]{:S(2)}) async-start(s32[4,64,16]{2,0,1:T(4,128)} %copy.33), calls=%async_computation | async-start | bytes 262144 | tf_op jit(solution)/shard_map/all_to_all | solution.py:109
  299.6 7.9 %all-to-all-done = s32[4,64,16]{2,0,1:T(4,128)S(1)} async-done(((s32[4,64,16]{2,0,1:T(4,128)}), s32[4,64,16]{2,0,1:T(4,128)S(1)}, u32[]{:S(2)}, u32[]{:S(2)}) %all-to-all-start) | async-done | bytes 16416 | tf_op jit(solution)/shard_map/all_to_all | solution.py:109
  307.5 5.6 all-to-all-start.1
  313.1 2.9 copy.38
  316.2 49.0 %all-to-all-done.1 = bf16[4,64,16,256]{3,2,0,1:T(8,128)(2,1)} async-done(((bf16[4,64,16,256]{3,2,0,1:T(8,128)(2,1)}), bf16[4,64,16,256]{3,2,0,1:T(8,128)(2,1)}, u32[]{:S(2)}, u32[]{:S(2)}) %all-to-all-start.1) | async-done | bytes 2097184 | tf_op jit(solution)/shard_map/all_to_all | solution.py:102
  367.0 2.9 multiply_reduce_fusion
  372.4 3.0 copy.49
  376.6 246.2 %psum.15 = f32[3,1024]{1,0:T(4,128)} all-reduce(f32[3,1024]{1,0:T(4,128)S(1)} %pad_maximum_fusion.1), channel_id=1, replica_groups=mesh['dp'=64,'mp'=4] {'dp'}, use_global_device_ids=true, to_apply=%region_15.0 | all-reduce | flops 3072 | bytes 24576 | tf_op jit(solution)/shard_map/psum | solution.py:200
  (124 shorter events, 49.4 us)
Async XLA Ops:
  7.2 289.3 %copy-start = (bf16[4,512,256]{2,1,0:T(8,128)(2,1)S(1)}, bf16[4,512,256]{2,1,0:T(8,128)(2,1)}, u32[]{:S(2)}) copy-start(bf16[4,512,256]{2,1,0:T(8,128)(2,1)} %param.15) | copy-start | bytes 3145732
  7.2 3.1 copy-start.23
  7.2 3.2 copy-start.22
  7.2 3.0 copy-start.15
  7.2 3.4 copy-start.16
  7.2 32.8 %copy-start.9 = (f32[4,512,256]{2,1,0:T(8,128)S(1)}, f32[4,512,256]{2,1,0:T(8,128)}, u32[]{:S(2)}) copy-start(f32[4,512,256]{2,1,0:T(8,128)} %param.13) | copy-start | bytes 6291460
  43.8 56.1 %all-to-all-start.3 = ((bf16[4,64,16,256]{3,2,0,1:T(8,128)(2,1)}), bf16[4,64,16,256]{3,2,0,1:T(8,128)(2,1)S(1)}, u32[]{:S(2)}, u32[]{:S(2)}) async-start(bf16[4,64,16,256]{3,2,0,1:T(8,128)(2,1)} %copy.45), calls=%async_computation.3 | async-start | bytes 4194304 | tf_op jit(solution)/shard_map/all_to_all | solution.py:144
  48.5 2.5 copy-start.20
  48.5 75.4 %reduce-scatter.6.cloned.1.call-start = ((), (), s32[]{:S(2)}) async-start(), calls=%async_computation.9 | async-start | bytes 655360 | tf_op jit(solution)/shard_map/reduce_scatter | solution.py:63
  103.4 61.9 %reduce-scatter.8.cloned.1.call-start = ((), (), s32[]{:S(2)}) async-start(), calls=%async_computation.10 | async-start | bytes 655360 | tf_op jit(solution)/shard_map/reduce_scatter | solution.py:63
  123.9 16.2 %copy-start.13 = (bf16[2,512,1024]{2,1,0:T(8,128)(2,1)S(1)}, bf16[2,512,1024]{2,1,0:T(8,128)(2,1)}, u32[]{:S(2)}) copy-start(bf16[2,512,1024]{2,1,0:T(8,128)(2,1)} %param.23) | copy-start | bytes 6291460
  137.3 4.1 copy-start.7
  140.1 41.3 %copy-start.4 = (bf16[256,1024]{1,0:T(8,128)(2,1)}, bf16[256,1024]{1,0:T(8,128)(2,1)S(1)}, u32[]{:S(2)}) copy-start(bf16[256,1024]{1,0:T(8,128)(2,1)S(1)} %get-tuple-element.48) | copy-start | bytes 1572868
  141.4 75.1 %reduce-scatter.10.cloned.1.call-start = ((), (), s32[]{:S(2)}) async-start(), calls=%async_computation.11 | async-start | bytes 655360 | tf_op jit(solution)/shard_map/reduce_scatter | solution.py:63
  166.2 23.5 %copy-start.21 = (s32[256]{0:T(256)S(1)}, s32[256]{0:T(256)}, u32[]{:S(2)}) copy-start(s32[256]{0:T(256)} %param.21) | copy-start | bytes 3076
  192.7 64.7 %reduce-scatter.12.cloned.1.call-start = ((), (), s32[]{:S(2)}) async-start(), calls=%async_computation.12 | async-start | bytes 655360 | tf_op jit(solution)/shard_map/reduce_scatter | solution.py:63
  216.5 15.7 %copy-start.3 = (bf16[2,512,1024]{2,1,0:T(8,128)(2,1)S(1)}, bf16[2,512,1024]{2,1,0:T(8,128)(2,1)}, u32[]{:S(2)}) copy-start(bf16[2,512,1024]{2,1,0:T(8,128)(2,1)} %param.22) | copy-start | bytes 6291460
  233.5 392.1 %reduce-scatter.14.cloned.1.call-start = ((), (), s32[]{:S(2)}) async-start(), calls=%async_computation.13 | async-start | bytes 8519680 | tf_op jit(solution)/shard_map/reduce_scatter | solution.py:33
  257.4 13.8 %copy-start.2 = (f32[1,512,1024]{2,1,0:T(8,128)S(1)}, f32[1,512,1024]{2,1,0:T(8,128)}, u32[]{:S(2)}) copy-start(f32[1,512,1024]{2,1,0:T(8,128)} %convolution_bitcast_fusion.2) | copy-start | bytes 6291460
  286.0 21.5 %all-to-all-start = ((s32[4,64,16]{2,0,1:T(4,128)}), s32[4,64,16]{2,0,1:T(4,128)S(1)}, u32[]{:S(2)}, u32[]{:S(2)}) async-start(s32[4,64,16]{2,0,1:T(4,128)} %copy.33), calls=%async_computation | async-start | bytes 262144 | tf_op jit(solution)/shard_map/all_to_all | solution.py:109
  307.5 57.6 %all-to-all-start.1 = ((bf16[4,64,16,256]{3,2,0,1:T(8,128)(2,1)}), bf16[4,64,16,256]{3,2,0,1:T(8,128)(2,1)}, u32[]{:S(2)}, u32[]{:S(2)}) async-start(bf16[4,64,16,256]{3,2,0,1:T(8,128)(2,1)} %copy.35), calls=%async_computation.1 | async-start | bytes 4194304 | tf_op jit(solution)/shard_map/all_to_all | solution.py:102
  366.9 2.9 copy-start.19
  367.0 3.5 copy-start.1
  372.4 250.5 %copy-start.6 = (f32[256,1024]{1,0:T(8,128)S(1)}, f32[256,1024]{1,0:T(8,128)}, u32[]{:S(2)}) copy-start(f32[256,1024]{1,0:T(8,128)} %get-tuple-element.50) | copy-start | bytes 3145732
  (8 other events, 11.8 us)
Sparse Core Ops, SparseCore 0:
  103.5 20.3 reduce-scatter.5
  141.5 23.7 reduce-scatter.7
  192.8 23.5 reduce-scatter.9
  233.7 23.7 reduce-scatter.11
  276.6 150.7 reduce-scatter.13
where the time goes:
time: 635 us; the launch traced here: 634 us
  blocking collectives  325 us (51%)
  waiting for transfers between devices  192 us (30%)
  local copies, waits for them, and re-layouts  34.7 us (5%)
  matrix products  31.7 us (5%)
  starting transfers between devices  21.1 us (3%)
  other arithmetic  15.5 us (2%)
  between operations  14.3 us (2%)
    psum x1, blocking collectives, local(): grad_small = lax.psum(jnp.stack(bias_grads + [head_grad]), 'dp')  246 us
    reduce_scatter x4, waiting for transfers between devices, summed_rounded(): share = lax.psum_scatter(partial, axis, scatter_dimension=0, tiled=True)  85.9 us
    all_gather x4, blocking collectives, summed_rounded(): return lax.all_gather(share.astype(jnp.bfloat16), axis, axis=0, tiled=True)  49 us
    all_to_all x1, waiting for transfers between devices, local(): lax.all_to_all(send_grads.reshape(local_feats, peers, grad_cap, width), '...  49 us
    all_to_all x1, waiting for transfers between devices, local(): lax.all_to_all(served.reshape(local_feats, peers, look_cap, width), 'dp',...  48.8 us
    unnamed x60, local copies, waits for them, and re-layouts  25.1 us
    all_to_all x1, blocking collectives, local(): lax.all_to_all(wanted.reshape(local_feats, peers, look_cap), 'dp', split_...  21.1 us
  transfers between devices with their start and end apart: 8, of which 7 were waited for; matrix products, arithmetic and copies ran while one was open for 6% of the time, Pallas kernels for 0%

commit v1 on v0

--- a/solution.py
+++ b/solution.py
@@ -197,7 +197,8 @@
     grad_u = jnp.stack(grads_u)
     grad_v = jnp.stack(grads_v)
     grad_u, grad_v = side_by_side((grad_u, grad_v), "dp", 1, 0)
-    grad_small = lax.psum(jnp.stack(bias_grads + [head_grad]), "dp")
+    in_array = jnp.stack(bias_grads + [head_grad])
+    grad_small = jnp.sum(lax.all_gather(in_array, axis_name="dp"), axis=0)
     grad_pooled = (upstream + to_start).astype(jnp.bfloat16)
     return (new_table, new_accum, grad_u, grad_v, grad_small, grad_pooled)
 

time: 635 us -> 448 us (0.71)
  blocking collectives: 325 us -> 133 us
    psum x1 -> x0, blocking collectives: 246 us -> none  [local(): grad_small = lax.psum(jnp.stack(bias_grads + [head_grad]), 'dp')]
    all_gather x0 -> x1, blocking collectives: none -> 54.5 us  [local(): grad_small = jnp.sum(lax.all_gather(in_array, axis_name='dp'), axis=0)]
  transfers between devices with their start and end apart: 8 -> 8, of which waited for: 7 -> 7; matrix products, arithmetic and copies ran while one was open for 6% -> 9% of each run, Pallas kernels for 0% -> 0%
where the time goes in v1:
time: 448 us; the launch traced here: 444 us
  waiting for transfers between devices  192 us (43%)
  blocking collectives  133 us (30%)
  local copies, waits for them, and re-layouts  34.6 us (8%)
  matrix products  31.7 us (7%)
  starting transfers between devices  21.1 us (5%)
  other arithmetic  17.6 us (4%)
  between operations  14.3 us (3%)
    reduce_scatter x4, waiting for transfers between devices, summed_rounded(): share = lax.psum_scatter(partial, axis, scatter_dimension=0, tiled=True)  85.9 us
    all_gather x1, blocking collectives, local(): grad_small = jnp.sum(lax.all_gather(in_array, axis_name='dp'), axis=0)  54.5 us
    all_gather x4, blocking collectives, summed_rounded(): return lax.all_gather(share.astype(jnp.bfloat16), axis, axis=0, tiled=True)  49 us
    all_to_all x1, waiting for transfers between devices, local(): lax.all_to_all(send_grads.reshape(local_feats, peers, grad_cap, width), '...  49 us
    all_to_all x1, waiting for transfers between devices, local(): lax.all_to_all(served.reshape(local_feats, peers, look_cap, width), 'dp',...  48.8 us
    unnamed x60, local copies, waits for them, and re-layouts  25 us
    all_to_all x1, blocking collectives, local(): lax.all_to_all(wanted.reshape(local_feats, peers, look_cap), 'dp', split_...  21.1 us
    all_to_all x1, starting transfers between devices, local(): lax.all_to_all(send_rows.reshape(local_feats, peers, grad_cap), 'dp', spl...  10.4 us
  transfers between devices with their start and end apart: 8, of which 7 were waited for; matrix products, arithmetic and copies ran while one was open for 9% of the time, Pallas kernels for 0%

profile of v1, /device:TPU:0, one launch (start us, length us, event | category | flops | bytes accessed | tf_op | source)
XLA Modules:
  0.0 444.1 jit_solution(10069818290897851126)
XLA Ops:
  10.6 8.1 %scatter_custom_fusion.1 = s32[4096]{0:T(1024)S(1)} fusion(s32[2048]{0:T(1024)S(1)} %bitcast.113, s32[2048]{0:T(1024)S(1)} %bitcast.115, s32[]{:T(128)} %constant.5.clone.1), kind=kCustom, calls=%fused_computation.105 | custom fusion | bytes 16388
  18.9 21.1 %all_to_all.20 = s32[4,64,16]{2,0,1:T(4,128)S(1)} all-to-all(s32[4,64,16]{2,0,1:T(4,128)S(1)} %copy.43), channel_id=1, replica_groups=mesh['dp'=64,'mp'=4] {'dp'}, dimensions={1} | all-to-all | bytes 32768 | tf_op jit(solution)/shard_map/all_to_all | solution.py:134
  43.8 4.7 %all-to-all-start.3 = ((bf16[4,64,16,256]{3,2,0,1:T(8,128)(2,1)}), bf16[4,64,16,256]{3,2,0,1:T(8,128)(2,1)S(1)}, u32[]{:S(2)}, u32[]{:S(2)}) async-start(bf16[4,64,16,256]{3,2,0,1:T(8,128)(2,1)} %copy.45), calls=%async_computation.3 | async-start | bytes 4194304 | tf_op jit(solution)/shard_map/all_to_all | solution.py:144
  51.0 48.8 %all-to-all-done.3 = bf16[4,64,16,256]{3,2,0,1:T(8,128)(2,1)S(1)} async-done(((bf16[4,64,16,256]{3,2,0,1:T(8,128)(2,1)}), bf16[4,64,16,256]{3,2,0,1:T(8,128)(2,1)S(1)}, u32[]{:S(2)}, u32[]{:S(2)}) %all-to-all-start.3) | async-done | bytes 2097184 | tf_op jit(solution)/shard_map/all_to_all | solution.py:144
  103.7 20.2 %reduce-scatter.6.cloned.1.call-done = f32[64,512]{1,0:T(8,128)} async-done(((f32[256,512]{1,0:T(8,128)}), f32[64,512]{1,0:T(8,128)}) %reduce-scatter.6.cloned.1.call-update) | async-done | bytes 131088 | tf_op jit(solution)/shard_map/reduce_scatter | solution.py:63
  125.0 12.3 %all_gather.18 = bf16[256,512]{1,0:T(8,128)(2,1)S(1)} all-gather(bf16[64,512]{1,0:T(8,128)(2,1)S(1)} %convert_element_type.138), channel_id=1, replica_groups=mesh['dp'=64,'mp'=4] {'mp'}, dimensions={0}, use_global_device_ids=true | all-gather | bytes 327680 | tf_op jit(solution)/shard_map/all_gather | solution.py:64
  141.5 23.9 %reduce-scatter.8.cloned.1.call-done = f32[64,512]{1,0:T(8,128)} async-done(((f32[256,512]{1,0:T(8,128)}), f32[64,512]{1,0:T(8,128)}) %reduce-scatter.8.cloned.1.call-update) | async-done | bytes 131088 | tf_op jit(solution)/shard_map/reduce_scatter | solution.py:63
  166.3 12.3 %all_gather.19 = bf16[256,512]{1,0:T(8,128)(2,1)S(1)} all-gather(bf16[64,512]{1,0:T(8,128)(2,1)S(1)} %convert_element_type.141), channel_id=1, replica_groups=mesh['dp'=64,'mp'=4] {'mp'}, dimensions={0}, use_global_device_ids=true | all-gather | bytes 327680 | tf_op jit(solution)/shard_map/all_gather | solution.py:64
  178.5 2.9 fusion.23
  181.4 8.4 %psum.7 = f32[256]{0:T(256)S(1)} all-reduce(f32[256]{0:T(256)S(1)} %get-tuple-element.28), channel_id=1, replica_groups=mesh['dp'=64,'mp'=4] {'mp'}, use_global_device_ids=true, to_apply=%region_8.0 | all-reduce | flops 256 | bytes 2048 | tf_op jit(solution)/shard_map/psum | solution.py:176
  192.8 23.7 %reduce-scatter.10.cloned.1.call-done = f32[64,512]{1,0:T(8,128)} async-done(((f32[256,512]{1,0:T(8,128)}), f32[64,512]{1,0:T(8,128)}) %reduce-scatter.10.cloned.1.call-update) | async-done | bytes 131088 | tf_op jit(solution)/shard_map/reduce_scatter | solution.py:63
  217.5 12.3 %all_gather.20 = bf16[256,512]{1,0:T(8,128)(2,1)S(1)} all-gather(bf16[64,512]{1,0:T(8,128)(2,1)S(1)} %convert_element_type.149), channel_id=1, replica_groups=mesh['dp'=64,'mp'=4] {'mp'}, dimensions={0}, use_global_device_ids=true | all-gather | bytes 327680 | tf_op jit(solution)/shard_map/all_gather | solution.py:64
  239.3 18.1 %reduce-scatter.12.cloned.1.call-done = f32[64,512]{1,0:T(8,128)} async-done(((f32[256,512]{1,0:T(8,128)}), f32[64,512]{1,0:T(8,128)}) %reduce-scatter.12.cloned.1.call-update) | async-done | bytes 131088 | tf_op jit(solution)/shard_map/reduce_scatter | solution.py:63
  258.5 12.3 %all_gather.21 = bf16[256,512]{1,0:T(8,128)(2,1)S(1)} all-gather(bf16[64,512]{1,0:T(8,128)(2,1)S(1)} %convert_element_type.152), channel_id=1, replica_groups=mesh['dp'=64,'mp'=4] {'mp'}, dimensions={0}, use_global_device_ids=true | all-gather | bytes 327680 | tf_op jit(solution)/shard_map/all_gather | solution.py:64
  271.3 5.2 %pad_maximum_fusion = f32[4,512,1024]{2,1,0:T(8,128)} fusion(f32[1,512,1024]{2,1,0:T(8,128)} %convolution_bitcast_fusion, f32[1,512,1024]{2,1,0:T(8,128)S(1)} %convolution_bitcast_fusion.1, f32[1,512,1024]{2,1,0:T(8,128)S(1)} %copy-done.2, f32[1,512,1024]{2,1,0:T(8,128)} %convolution_bitcast_fusion.3), kind=kLoop, calls=%fused_computation.2 | loop fusion | flops 6291456 | bytes 16777216 | tf_op jit(solution)/shard_map/concatenate | solution.py:32
  277.2 8.1 %scatter_custom_fusion = s32[4096]{0:T(1024)S(1)} fusion(s32[2048]{0:T(1024)S(1)} %bitcast.114, s32[2048]{0:T(1024)S(1)} %bitcast.116, s32[]{:T(128)} %constant.11.clone.1), kind=kCustom, calls=%fused_computation.107 | custom fusion | bytes 16388
  286.1 10.4 %all-to-all-start = ((s32[4,64,16]{2,0,1:T(4,128)}), s32[4,64,16]{2,0,1:T(4,128)S(1)}, u32[]{:S(2)}, u32[]{:S(2)}) async-start(s32[4,64,16]{2,0,1:T(4,128)} %copy.33), calls=%async_computation | async-start | bytes 262144 | tf_op jit(solution)/shard_map/all_to_all | solution.py:109
  299.6 7.9 %all-to-all-done = s32[4,64,16]{2,0,1:T(4,128)S(1)} async-done(((s32[4,64,16]{2,0,1:T(4,128)}), s32[4,64,16]{2,0,1:T(4,128)S(1)}, u32[]{:S(2)}, u32[]{:S(2)}) %all-to-all-start) | async-done | bytes 16416 | tf_op jit(solution)/shard_map/all_to_all | solution.py:109
  307.6 5.6 %all-to-all-start.1 = ((bf16[4,64,16,256]{3,2,0,1:T(8,128)(2,1)}), bf16[4,64,16,256]{3,2,0,1:T(8,128)(2,1)}, u32[]{:S(2)}, u32[]{:S(2)}) async-start(bf16[4,64,16,256]{3,2,0,1:T(8,128)(2,1)} %copy.35), calls=%async_computation.1 | async-start | bytes 4194304 | tf_op jit(solution)/shard_map/all_to_all | solution.py:102
  313.1 2.9 copy.38
  316.2 49.0 %all-to-all-done.1 = bf16[4,64,16,256]{3,2,0,1:T(8,128)(2,1)} async-done(((bf16[4,64,16,256]{3,2,0,1:T(8,128)(2,1)}), bf16[4,64,16,256]{3,2,0,1:T(8,128)(2,1)}, u32[]{:S(2)}, u32[]{:S(2)}) %all-to-all-start.1) | async-done | bytes 2097184 | tf_op jit(solution)/shard_map/all_to_all | solution.py:102
  367.0 2.9 multiply_reduce_fusion
  372.4 2.9 copy.49
  376.7 54.5 %all-gather.1 = f32[64,3,1024]{2,1,0:T(4,128)} all-gather(f32[1,3,1024]{2,1,0:T(4,128)S(1)} %maximum_bitcast_fusion), channel_id=2, replica_groups=mesh['dp'=64,'mp'=4] {'dp'}, dimensions={0}, use_global_device_ids=true | all-gather | bytes 798720 | tf_op jit(solution)/shard_map/all_gather | solution.py:201
  (125 shorter events, 51.5 us)
Async XLA Ops:
  7.2 289.4 %copy-start = (bf16[4,512,256]{2,1,0:T(8,128)(2,1)S(1)}, bf16[4,512,256]{2,1,0:T(8,128)(2,1)}, u32[]{:S(2)}) copy-start(bf16[4,512,256]{2,1,0:T(8,128)(2,1)} %param.15) | copy-start | bytes 3145732
  7.2 3.1 copy-start.23
  7.2 3.2 copy-start.22
  7.2 3.0 copy-start.15
  7.2 3.4 copy-start.16
  7.2 32.8 %copy-start.9 = (f32[4,512,256]{2,1,0:T(8,128)S(1)}, f32[4,512,256]{2,1,0:T(8,128)}, u32[]{:S(2)}) copy-start(f32[4,512,256]{2,1,0:T(8,128)} %param.13) | copy-start | bytes 6291460
  43.8 56.1 %all-to-all-start.3 = ((bf16[4,64,16,256]{3,2,0,1:T(8,128)(2,1)}), bf16[4,64,16,256]{3,2,0,1:T(8,128)(2,1)S(1)}, u32[]{:S(2)}, u32[]{:S(2)}) async-start(bf16[4,64,16,256]{3,2,0,1:T(8,128)(2,1)} %copy.45), calls=%async_computation.3 | async-start | bytes 4194304 | tf_op jit(solution)/shard_map/all_to_all | solution.py:144
  48.5 2.5 copy-start.20
  48.5 75.4 %reduce-scatter.6.cloned.1.call-start = ((), (), s32[]{:S(2)}) async-start(), calls=%async_computation.9 | async-start | bytes 655360 | tf_op jit(solution)/shard_map/reduce_scatter | solution.py:63
  103.4 61.9 %reduce-scatter.8.cloned.1.call-start = ((), (), s32[]{:S(2)}) async-start(), calls=%async_computation.10 | async-start | bytes 655360 | tf_op jit(solution)/shard_map/reduce_scatter | solution.py:63
  123.9 16.2 %copy-start.13 = (bf16[2,512,1024]{2,1,0:T(8,128)(2,1)S(1)}, bf16[2,512,1024]{2,1,0:T(8,128)(2,1)}, u32[]{:S(2)}) copy-start(bf16[2,512,1024]{2,1,0:T(8,128)(2,1)} %param.23) | copy-start | bytes 6291460
  137.3 4.1 copy-start.7
  140.1 41.3 %copy-start.4 = (bf16[256,1024]{1,0:T(8,128)(2,1)}, bf16[256,1024]{1,0:T(8,128)(2,1)S(1)}, u32[]{:S(2)}) copy-start(bf16[256,1024]{1,0:T(8,128)(2,1)S(1)} %get-tuple-element.48) | copy-start | bytes 1572868
  141.4 75.1 %reduce-scatter.10.cloned.1.call-start = ((), (), s32[]{:S(2)}) async-start(), calls=%async_computation.11 | async-start | bytes 655360 | tf_op jit(solution)/shard_map/reduce_scatter | solution.py:63
  166.2 23.5 %copy-start.21 = (s32[256]{0:T(256)S(1)}, s32[256]{0:T(256)}, u32[]{:S(2)}) copy-start(s32[256]{0:T(256)} %param.21) | copy-start | bytes 3076
  192.7 64.7 %reduce-scatter.12.cloned.1.call-start = ((), (), s32[]{:S(2)}) async-start(), calls=%async_computation.12 | async-start | bytes 655360 | tf_op jit(solution)/shard_map/reduce_scatter | solution.py:63
  216.5 15.7 %copy-start.3 = (bf16[2,512,1024]{2,1,0:T(8,128)(2,1)S(1)}, bf16[2,512,1024]{2,1,0:T(8,128)(2,1)}, u32[]{:S(2)}) copy-start(bf16[2,512,1024]{2,1,0:T(8,128)(2,1)} %param.22) | copy-start | bytes 6291460
  233.5 202.5 %reduce-scatter.14.cloned.1.call-start = ((), (), s32[]{:S(2)}) async-start(), calls=%async_computation.13 | async-start | bytes 8519680 | tf_op jit(solution)/shard_map/reduce_scatter | solution.py:33
  257.4 13.8 %copy-start.2 = (f32[1,512,1024]{2,1,0:T(8,128)S(1)}, f32[1,512,1024]{2,1,0:T(8,128)}, u32[]{:S(2)}) copy-start(f32[1,512,1024]{2,1,0:T(8,128)} %convolution_bitcast_fusion.2) | copy-start | bytes 6291460
  286.1 21.5 %all-to-all-start = ((s32[4,64,16]{2,0,1:T(4,128)}), s32[4,64,16]{2,0,1:T(4,128)S(1)}, u32[]{:S(2)}, u32[]{:S(2)}) async-start(s32[4,64,16]{2,0,1:T(4,128)} %copy.33), calls=%async_computation | async-start | bytes 262144 | tf_op jit(solution)/shard_map/all_to_all | solution.py:109
  307.6 57.6 %all-to-all-start.1 = ((bf16[4,64,16,256]{3,2,0,1:T(8,128)(2,1)}), bf16[4,64,16,256]{3,2,0,1:T(8,128)(2,1)}, u32[]{:S(2)}, u32[]{:S(2)}) async-start(bf16[4,64,16,256]{3,2,0,1:T(8,128)(2,1)} %copy.35), calls=%async_computation.1 | async-start | bytes 4194304 | tf_op jit(solution)/shard_map/all_to_all | solution.py:102
  367.0 2.9 copy-start.19
  367.0 3.5 copy-start.1
  375.3 57.9 %copy-start.6 = (f32[256,1024]{1,0:T(8,128)S(1)}, f32[256,1024]{1,0:T(8,128)}, u32[]{:S(2)}) copy-start(f32[256,1024]{1,0:T(8,128)} %get-tuple-element.50) | copy-start | bytes 3145732
  (8 other events, 11.8 us)
Sparse Core Ops, SparseCore 0:
  103.5 20.3 reduce-scatter.5
  141.5 23.7 reduce-scatter.7
  192.8 23.5 reduce-scatter.9
  233.7 23.7 reduce-scatter.11
  276.6 151.3 reduce-scatter.13
